TPU v7x, 256 devices: a whole 4x4x8 slice. The times are simulated.
256 devices in a mesh: req: 64 (over z, x, core), tp: 4 (over y).
Axes of the slice: x: 4, y: 4, z: 8, core: 2. Of those that a mesh axis runs over, the one named last changes fastest.
Arguments:
- layer_in: bfloat16 [8192, 2880], P('req', 'tp'), may hold values from -6 to 6
- queries: bfloat16 [8192, 4096], P('req', 'tp'), may hold values from -32 to 32
- key_values: bfloat16 [8192, 2, 512], P('req', None, 'tp'), may hold values from -12 to 12
- prefix_cache: bfloat16 [4, 1024, 2, 512], P(None, 'req', None, 'tp'), may hold values from -8 to 8
- sink_logits: float32 [64], P('tp'), may hold values from 8 to 12
- lengths: int32 [512], P('req'), may hold values from 1 to 16
- groups: int32 [512], P('req'), may hold values from 0 to 3
- batch_home: int32 [64], replicated, may hold values from 0 to 63, each once
- expert_ids: int32 [8192, 4], P('req'), may hold values from 0 to 31, all different within a row; in each aligned block of 128 rows (0 to 127, 128 to 255, ...) at most 24 rows name the same one
- router_logits: float32 [8192, 4], P('req'), may hold values from -6 to 6
- norm_gain: float32 [2880], replicated, may hold values from 0.1 to 1.9
- output_weight: bfloat16 [4096, 2880], P('tp'), may hold values from -0.09375 to 0.09375
- gate_up: bfloat16 [64, 2880, 2, 1440], P('req', None, None, 'tp'), may hold values from -0.109375 to 0.109375
- expert_down: bfloat16 [64, 1440, 2880], P('req', 'tp'), may hold values from -0.109375 to 0.109375
Outputs:
- layer_out: bfloat16 [8192, 2880], P('req', 'tp')
Inputs may be any that keep to these rules, and one draw needn't show every extreme that they name: `expert_ids`: in the token slots of one index of req, no expert is named by more than 24 slots. `batch_home`: A permutation.
All inputs are finite; a program needn't handle non-finite values.
Results may differ from a plain program's by a relative error of at most 0.017.
Values may be sent and summed in bfloat16 or wider, within the bound.
No kernel may reach another device: no remote copies, remote signals or barrier semaphores. Data moves between devices by JAX's collectives and lax.ppermute only.
A program may use at most 192 MiB of HBM per device.

v0:
```python
import jax
import jax.numpy as jnp
from jax import lax
from jax.sharding import PartitionSpec as P

D = 2880
HD = 64
EXPERTS = 32
TOPK = 4
PREFIX = 1024
CAP = 24


theta_base = 150000.0
norm_eps = 1e-05
logit_scale = 0.125
masked_score = -1e30


def rotate(values, positions):
    middle = values.shape[-1] // 2
    lane_index = jnp.arange(middle, dtype=jnp.int32).astype(jnp.float32)
    inverse_freq = theta_base ** (-2.0 * lane_index / values.shape[-1])
    angles = positions.astype(jnp.float32)[:, None] * inverse_freq[None, :]
    cosine = jnp.cos(angles)[:, None, :]
    sine_part = jnp.sin(angles)[:, None, :]
    front_half = values[..., :middle]
    back_half = values[..., middle:]
    return jnp.concatenate(
        [front_half * cosine - back_half * sine_part, back_half * cosine + front_half * sine_part],
        axis=-1,
    )


def absorb_block(softmax_state, query_groups, block_keys, block_values, allowed):
    run_max, run_sum, run_acc = softmax_state
    score_matrix = (
        jnp.einsum(
            "rskgd,rbkd->rskgb", query_groups, block_keys, preferred_element_type=jnp.float32
        )
        * logit_scale
    )
    if allowed is not None:
        score_matrix = jnp.where(allowed, score_matrix, masked_score)
    new_max = jnp.maximum(run_max, jnp.max(score_matrix, axis=-1))
    rescale = jnp.exp(run_max - new_max)
    weights = jnp.exp(score_matrix - new_max[..., None])
    new_sum = run_sum * rescale + jnp.sum(weights, axis=-1)
    new_acc = run_acc * rescale[..., None] + jnp.einsum(
        "rskgb,rbkd->rskgd",
        weights.astype(jnp.bfloat16),
        block_values,
        preferred_element_type=jnp.float32,
    )
    return (new_max, new_sum, new_acc)


def body(
    layer_in,
    queries,
    key_values,
    prefix_cache,
    sink_logits,
    lengths,
    groups,
    batch_home,
    expert_ids,
    router_logits,
    norm_gain,
    output_weight,
    gate_up,
    expert_down,
):
    tokens = queries.shape[0]
    requests = lengths.shape[0]
    suffix = tokens // requests
    local_heads = sink_logits.shape[0]
    kv_local = key_values.shape[2] // HD
    per_group = local_heads // kv_local
    slot_index = jnp.tile(jnp.arange(suffix, dtype=jnp.int32), requests)
    positions = PREFIX + slot_index
    rotated_queries = rotate(
        queries.reshape(tokens, local_heads, HD).astype(jnp.float32), positions
    ).astype(jnp.bfloat16)
    query_groups = rotated_queries.reshape(requests, suffix, kv_local, per_group, HD)
    fresh_keys = rotate(
        key_values[:, 0].reshape(tokens, kv_local, HD).astype(jnp.float32), positions
    ).astype(jnp.bfloat16)
    fresh_keys = fresh_keys.reshape(requests, suffix, kv_local, HD)
    fresh_values = key_values[:, 1].reshape(requests, suffix, kv_local, HD)
    sink_values = sink_logits.reshape(kv_local, per_group)
    state_shape = (requests, suffix, kv_local, per_group)
    start_state = (
        jnp.broadcast_to(sink_values[None, None], state_shape),
        jnp.ones(state_shape, jnp.float32),
        jnp.zeros(state_shape + (HD,), jnp.float32),
    )
    page_rows = lax.all_gather(prefix_cache, "req", axis=1, tiled=True)
    span_rows = page_rows.shape[1]
    block_rows = 512
    chosen = page_rows[groups]
    stacked = chosen.reshape(requests, span_rows // block_rows, block_rows, 2, kv_local, HD)

    def absorb_one(inner_state, block_index):
        block_pair = lax.dynamic_index_in_dim(stacked, block_index, 1, keepdims=False)
        return (
            absorb_block(inner_state, query_groups, block_pair[:, :, 0], block_pair[:, :, 1], None),
            None,
        )

    final_state, _ = lax.scan(absorb_one, start_state, jnp.arange(span_rows // block_rows))
    local_pos = jnp.arange(suffix, dtype=jnp.int32)
    causal = local_pos[None, :] <= local_pos[:, None]
    within = local_pos[None, None, :] < lengths[:, None, None]
    allowed = (causal[None] & within)[:, :, None, None, :]
    run_max, run_sum, run_acc = absorb_block(
        final_state, query_groups, fresh_keys, fresh_values, allowed
    )
    attention = (
        (run_acc / run_sum[..., None]).reshape(tokens, local_heads * HD).astype(jnp.bfloat16)
    )
    partial_value = jnp.dot(attention, output_weight, preferred_element_type=jnp.float32)
    tp_index = lax.axis_index("tp")
    quarter_cols = D // lax.axis_size("tp")
    placed = lax.dynamic_update_slice_in_dim(
        jnp.zeros((tokens, D), jnp.float32),
        layer_in.astype(jnp.float32),
        tp_index * quarter_cols,
        1,
    )
    residual = lax.psum((partial_value + placed).astype(jnp.bfloat16), "tp")
    live_rows = slot_index < jnp.repeat(lengths, suffix)
    pair_weight = jnp.where(live_rows[:, None], jax.nn.softmax(router_logits, axis=-1), 0.0).astype(
        jnp.bfloat16
    )
    flat_ids = expert_ids.reshape(-1)
    onehot = (flat_ids[:, None] == jnp.arange(EXPERTS, dtype=jnp.int32)[None, :]).astype(jnp.int32)
    before = jnp.cumsum(onehot, axis=0) - onehot
    rank_in = jnp.sum(before * onehot, axis=1)
    flat_slot = flat_ids * CAP + rank_in
    pair_token = jnp.arange(tokens * TOPK, dtype=jnp.int32) // TOPK
    token_table = (
        jnp.full((EXPERTS * CAP,), tokens, dtype=jnp.int32)
        .at[flat_slot]
        .set(pair_token)
        .reshape(EXPERTS, CAP)
    )
    weight_table = (
        jnp.zeros((EXPERTS * CAP,), jnp.bfloat16)
        .at[flat_slot]
        .set(pair_weight.reshape(-1))
        .reshape(EXPERTS, CAP)
    )
    devices_req = lax.axis_size("req")
    slab_count = gate_up.shape[0]
    split_count = devices_req * slab_count // EXPERTS
    slab_ids = jnp.arange(devices_req * slab_count, dtype=jnp.int32).reshape(
        devices_req, slab_count
    )
    expert_of = slab_ids // split_count
    token_send = token_table[expert_of]
    weight_send = weight_table[expert_of]
    padded = jnp.concatenate([residual, jnp.zeros((1, residual.shape[1]), jnp.bfloat16)], axis=0)
    rows_send = padded[token_send]
    device_range = jnp.arange(devices_req, dtype=jnp.int32)
    inverse = jnp.sum(
        device_range[:, None] * (batch_home[:, None] == device_range[None, :]).astype(jnp.int32),
        axis=0,
    )
    first_copy = (
        (lax.axis_index("req") * slab_count + jnp.arange(slab_count, dtype=jnp.int32)) % split_count
        == 0
    ).astype(jnp.float32)
    rows_in = lax.all_to_all(rows_send, "req", split_axis=0, concat_axis=0, tiled=True)
    arrived_weight = lax.all_to_all(weight_send, "req", split_axis=0, concat_axis=0, tiled=True)
    arrived_token = lax.all_to_all(token_send, "req", split_axis=0, concat_axis=0, tiled=True)
    rows_float = rows_in.astype(jnp.float32)
    row_scale = lax.rsqrt(jnp.mean(rows_float * rows_float, axis=-1, keepdims=True) + norm_eps)
    normed = (rows_float * row_scale * norm_gain).astype(jnp.bfloat16)
    gate_and_up = jnp.einsum(
        "njcd,jdgf->njcgf", normed, gate_up, preferred_element_type=jnp.float32
    )
    hidden = (jax.nn.silu(gate_and_up[..., 0, :]) * gate_and_up[..., 1, :]).astype(jnp.bfloat16)
    partial_out = jnp.einsum(
        "njcf,jfd->njcd", hidden, expert_down, preferred_element_type=jnp.float32
    )
    value_total = lax.psum_scatter(
        partial_out.astype(jnp.bfloat16), "tp", scatter_dimension=3, tiled=True
    ).astype(jnp.float32)
    own_rows = lax.dynamic_slice_in_dim(rows_float, tp_index * quarter_cols, quarter_cols, 3)
    result = (
        arrived_weight.astype(jnp.float32)[..., None]
        * (value_total + first_copy[None, :, None, None] * own_rows)
    ).astype(jnp.bfloat16)
    moved = result[inverse]
    moved_token = arrived_token[inverse]
    returned = lax.all_to_all(moved, "req", split_axis=0, concat_axis=0, tiled=True)
    returned_token = lax.all_to_all(moved_token, "req", split_axis=0, concat_axis=0, tiled=True)
    flat_rows = returned.reshape(-1, quarter_cols)
    flat_token = returned_token.reshape(-1)
    selector = (jnp.arange(tokens, dtype=jnp.int32)[:, None] == flat_token[None, :]).astype(
        jnp.bfloat16
    )
    return jnp.dot(selector, flat_rows, preferred_element_type=jnp.float32).astype(jnp.bfloat16)


def solution(mesh):
    placed = (
        P("req", "tp"),
        P("req", "tp"),
        P("req", None, "tp"),
        P(None, "req", None, "tp"),
        P("tp"),
        P("req"),
        P("req"),
        P(),
        P("req", None),
        P("req", None),
        P(),
        P("tp", None),
        P("req", None, None, "tp"),
        P("req", "tp", None),
    )
    return jax.shard_map(
        body, mesh=mesh, in_specs=placed, out_specs=P("req", "tp"), check_vma=False
    )
```

profile of v0, /device:TPU:2, one launch (start us, length us, event | category | flops | bytes accessed | tf_op | source)
XLA Modules:
  0.0 776.3 jit_solution(6258052218255485450)
XLA Ops:
  28.8 56.3 %all-gather.2.cloned.1.call-done = bf16[4,1024,2,128]{3,2,1,0:T(2,128)(2,1)} async-done(((bf16[4,16,2,128]{3,2,1,0:T(2,128)(2,1)}), bf16[4,1024,2,128]{3,2,1,0:T(2,128)(2,1)}) %all-gather.2.cloned.1.call-update) | async-done | bytes 2097168 | tf_op jit(solution)/shard_map/all_gather | solution.py:98
  85.1 11.4 %gather_fusion.3 = bf16[8,1024,2,128]{3,2,1,0:T(2,128)(2,1)} fusion(bf16[4,1024,2,128]{3,2,1,0:T(2,128)(2,1)} %all-gather.2.cloned.1.call-done, s32[1024]{0:T(1024)S(1)} %pad_clamp_fusion.1), kind=kCustom, calls=%fused_computation.3 | custom fusion | bytes 8388640 | tf_op jit(solution)/shard_map/gather | solution.py:101
  96.5 17.5 %reshape.462 = bf16[8,2,512,2,2,64]{5,4,3,2,1,0:T(2,128)(2,1)} reshape(bf16[8,1024,2,128]{3,2,1,0:T(2,128)(2,1)} %gather_fusion.3) | data formatting | bytes 8388608 | tf_op jit(solution)/shard_map/reshape | solution.py:102
  114.0 20.0 %copy.79 = bf16[8,2,512,2,2,64]{2,5,4,0,3,1:T(8,128)(2,1)} copy(bf16[8,2,512,2,2,64]{5,4,3,2,1,0:T(2,128)(2,1)} %reshape.462) | data formatting | bytes 8388608
  134.1 26.8 %while.15 = (s32[]{:T(128)}, f32[8,16,2,8]{1,3,2,0:T(8,128)S(1)}, f32[8,16,2,8]{1,3,2,0:T(8,128)S(1)}, f32[8,16,2,8,64]{4,1,3,2,0:T(8,128)S(1)}, s32[2]{0:T(128)...) while((s32[]{:T(128)}, f32[8,16,2,8]{1,3,2,0:T(8,128)S(1)}, ...), condition=%wide.region_11.12_spmd.clone, body=%wide.region_8.11_spmd.clone.sunk | while | flops 277223424 | bytes 46792948 | solution.py:111
  175.4 43.8 %all-reduce.3.cloned.1.call-done = bf16[128,2880]{0,1:T(8,128)(2,1)} async-done(((bf16[128,2880]{0,1:T(8,128)(2,1)}), bf16[128,2880]{0,1:T(8,128)(2,1)}) %all-reduce.3.cloned.1.call-update) | async-done | bytes 737296 | tf_op jit(solution)/shard_map/psum | solution.py:131
  222.7 8.1 %gather_fusion.4 = bf16[1536,2880]{1,0:T(8,128)(2,1)} fusion(bf16[129,2880]{1,0:T(8,128)(2,1)S(1)} %concatenate.27.clone, s32[2048]{0:T(1024)S(1)} %pad_clamp_fusion), kind=kCustom, calls=%fused_computation.4 | custom fusion | bytes 17700864 | tf_op jit(solution)/shard_map/gather | solution.py:164
  230.8 210.6 %all_to_all.25 = bf16[64,1,24,2880]{3,2,1,0:T(8,128)(2,1)S(1)} all-to-all(bf16[64,1,24,2880]{3,2,1,0:T(8,128)(2,1)} %bitcast.180), channel_id=1, replica_groups=mesh['req'=64,'tp'=4] {'req'}, dimensions={0} | all-to-all | bytes 17694720 | tf_op jit(solution)/shard_map/all_to_all | solution.py:174
  444.9 10.1 %fusion.25 = f32[64,1,24,2,360]{4,2,3,0,1:T(8,128)S(1)} fusion(bf16[1,2880,2,360]{1,3,2,0:T(8,128)(2,1)} %param.28, f32[2880]{0:T(1024)S(1)} %copy-done.12, f32[64,24]{1,0:T(8,128)S(1)} %add_rsqrt_fusion, bf16[64,1,24,2880]{3,2,1,0:T(8,128)(2,1)S(1)} %all_to_all.25), kind=kOutput, calls=%fused_computation.40 | convolution fusion | flops 6387793920 | bytes 17435904 | tf_op jit(solution)/shard_map/njcd,jdgf->njcgf/dot_general | solution.py:180
  455.1 7.7 convert_bitcast_fusion
  462.7 42.9 %copy.105 = bf16[64,1,24,2880]{2,0,1,3:T(8,128)(2,1)} copy(bf16[64,1,24,2880]{3,2,0,1:T(8,128)(2,1)} %convert_bitcast_fusion) | data formatting | bytes 17694720
  505.7 64.7 %reshape.463 = bf16[2880,1536]{1,0:T(8,128)(2,1)} reshape(bf16[2880,1,64,24]{3,2,1,0:T(8,128)(2,1)} %bitcast.178) | data formatting | bytes 17694720
  576.6 5.8 all-to-all-start.2
  582.5 8.5 %all-to-all-done.2 = bf16[64,1,24]{2,1,0:T(2,128)(2,1)S(1)} async-done(((bf16[64,1,24]{2,1,0:T(2,128)(2,1)}), bf16[64,1,24]{2,1,0:T(2,128)(2,1)S(1)}, u32[]{:S(2)}, u32[]{:S(2)}) %all-to-all-start.2) | async-done | bytes 3104 | tf_op jit(solution)/shard_map/all_to_all | solution.py:175
  591.0 5.5 all-to-all-start
  596.6 8.6 %all-to-all-done = s32[64,1,24]{2,1,0:T(1,128)S(1)} async-done(((s32[64,1,24]{2,1,0:T(1,128)}), s32[64,1,24]{2,1,0:T(1,128)S(1)}, u32[]{:S(2)}, u32[]{:S(2)}) %all-to-all-start) | async-done | bytes 6176 | tf_op jit(solution)/shard_map/all_to_all | solution.py:176
  606.3 5.9 all-to-all-start.1
  612.2 11.5 %convert_element_type.160 = f32[64,1,24,2880]{3,2,1,0:T(8,128)} convert(bf16[64,1,24,2880]{3,2,1,0:T(8,128)(2,1)} %copy-done.3) | non-fusion elementwise | flops 4423680 | bytes 26542080 | tf_op jit(solution)/shard_map/convert_element_type | solution.py:177
  623.7 29.6 %reduce-scatter.4.cloned.1.call-done = bf16[720,1536]{1,0:T(8,128)(2,1)} async-done(((bf16[2880,1536]{1,0:T(8,128)(2,1)}), bf16[720,1536]{1,0:T(8,128)(2,1)}) %reduce-scatter.4.cloned.1.call-update) | async-done | bytes 2211856
  653.3 21.0 %reshape.464 = bf16[720,1,64,24]{3,2,1,0:T(8,128)(2,1)} reshape(bf16[720,1536]{1,0:T(8,128)(2,1)} %reduce-scatter.4.cloned.1.call-done) | data formatting | bytes 4423680
  674.2 14.0 %copy.106 = bf16[64,1,24,720]{3,2,0,1:T(8,128)(2,1)} copy(bf16[64,1,24,720]{2,0,1,3:T(8,128)(2,1)} %bitcast.179) | data formatting | bytes 4423680
  688.2 6.4 fusion.23
  698.4 10.7 %all-to-all-start.4 = ((bf16[64,1,24,720]{3,2,1,0:T(8,128)(2,1)}), bf16[64,1,24,720]{3,2,1,0:T(8,128)(2,1)}, u32[]{:S(2)}, u32[]{:S(2)}) async-start(bf16[64,1,24,720]{3,2,1,0:T(8,128)(2,1)} %bitcast.181), calls=%async_computation.4 | async-start | bytes 4718592 | tf_op jit(solution)/shard_map/all_to_all | solution.py:197
  710.5 55.5 %all-to-all-done.4 = bf16[64,1,24,720]{3,2,1,0:T(8,128)(2,1)} async-done(((bf16[64,1,24,720]{3,2,1,0:T(8,128)(2,1)}), bf16[64,1,24,720]{3,2,1,0:T(8,128)(2,1)}, u32[]{:S(2)}, u32[]{:S(2)}) %all-to-all-start.4) | async-done | bytes 2211872 | tf_op jit(solution)/shard_map/all_to_all | solution.py:197
  (148 shorter events, 81.8 us)
Async XLA Ops:
  6.5 448.5 %copy-start = (bf16[1,360,2880]{2,1,0:T(8,128)(2,1)S(1)}, bf16[1,360,2880]{2,1,0:T(8,128)(2,1)}, u32[]{:S(2)}) copy-start(bf16[1,360,2880]{2,1,0:T(8,128)(2,1)} %param.29) | copy-start | bytes 6220804
  6.5 17.1 %copy-start.9 = (s32[128,4]{0,1:T(4,128)S(1)}, s32[128,4]{0,1:T(4,128)}, u32[]{:S(2)}) copy-start(s32[128,4]{0,1:T(4,128)} %param.24) | copy-start | bytes 6148
  6.5 12.9 %copy-start.6 = (bf16[128,2,128]{2,1,0:T(2,128)(2,1)S(1)}, bf16[128,2,128]{2,1,0:T(2,128)(2,1)}, u32[]{:S(2)}) copy-start(bf16[128,2,128]{2,1,0:T(2,128)(2,1)} %param.18) | copy-start | bytes 196612
  6.5 14.1 %copy-start.13 = (f32[16]{0:T(128)S(1)}, f32[16]{0:T(128)}, u32[]{:S(2)}) copy-start(f32[16]{0:T(128)} %param.20) | copy-start | bytes 196
  6.5 17.4 %copy-start.14 = (s32[8]{0:T(128)S(1)}, s32[8]{0:T(128)}, u32[]{:S(2)}) copy-start(s32[8]{0:T(128)} %param.22) | copy-start | bytes 100
  6.5 78.6 %all-gather.2.cloned.1.call-start = ((), (), s32[]{:S(2)}) async-start(), calls=%async_computation.6 | async-start | bytes 2129920 | tf_op jit(solution)/shard_map/all_gather | solution.py:98
  7.3 212.0 %all-reduce.3.cloned.1.call-start = ((), (), s32[]{:S(2)}) async-start(), calls=%async_computation.7 | async-start | bytes 1474560 | tf_op jit(solution)/shard_map/psum | solution.py:131
  8.4 17.1 %copy-start.15 = (s32[8]{0:T(128)S(1)}, s32[8]{0:T(128)}, u32[]{:S(2)}) copy-start(s32[8]{0:T(128)} %param.21) | copy-start | bytes 100
  25.6 0.8 copy-start.4
  136.8 3.2 copy-start.5
  138.7 1.3 copy-start.2
  140.8 1.9 copy-start.1
  150.2 3.2 copy-start.5
  152.1 1.3 copy-start.2
  154.2 1.9 copy-start.1
  165.1 4.4 copy-start.7
  170.5 482.7 %reduce-scatter.4.cloned.1.call-start = ((), (), s32[]{:S(2)}) async-start(), calls=%async_computation.8 | async-start | bytes 11059200
  441.5 3.4 copy-start.3
  441.5 3.4 copy-start.12
  570.4 12.0 %copy-start.16 = (s32[64]{0:T(128)S(1)}, s32[64]{0:T(128)}, u32[]{:S(2)}) copy-start(s32[64]{0:T(128)} %param.23) | copy-start | bytes 772
  576.6 14.4 %all-to-all-start.2 = ((bf16[64,1,24]{2,1,0:T(2,128)(2,1)}), bf16[64,1,24]{2,1,0:T(2,128)(2,1)S(1)}, u32[]{:S(2)}, u32[]{:S(2)}) async-start(bf16[64,1,24]{2,1,0:T(2,128)(2,1)} %copy.72), calls=%async_computation.2 | async-start | bytes 65536 | tf_op jit(solution)/shard_map/all_to_all | solution.py:175
  591.0 14.2 %all-to-all-start = ((s32[64,1,24]{2,1,0:T(1,128)}), s32[64,1,24]{2,1,0:T(1,128)S(1)}, u32[]{:S(2)}, u32[]{:S(2)}) async-start(s32[64,1,24]{2,1,0:T(1,128)} %bitcast.5), calls=%async_computation | async-start | bytes 65536 | tf_op jit(solution)/shard_map/all_to_all | solution.py:176
  606.3 92.1 %all-to-all-start.1 = ((s32[64,1,24]{2,1,0:T(1,128)}), s32[64,1,24]{2,1,0:T(1,128)S(1)}, u32[]{:S(2)}, u32[]{:S(2)}) async-start(s32[64,1,24]{2,1,0:T(1,128)} %bitcast.10), calls=%async_computation.1 | async-start | bytes 65536 | tf_op jit(solution)/shard_map/all_to_all | solution.py:198
  698.4 67.5 %all-to-all-start.4 = ((bf16[64,1,24,720]{3,2,1,0:T(8,128)(2,1)}), bf16[64,1,24,720]{3,2,1,0:T(8,128)(2,1)}, u32[]{:S(2)}, u32[]{:S(2)}) async-start(bf16[64,1,24,720]{3,2,1,0:T(8,128)(2,1)} %bitcast.181), calls=%async_computation.4 | async-start | bytes 4718592 | tf_op jit(solution)/shard_map/all_to_all | solution.py:197
  (3 other events, 2.0 us)
Sparse Core Ops, SparseCore 0:
  10.0 75.0 all-gather.1
  170.6 48.5 all-reduce.2
  570.5 82.6 reduce-scatter.3
where the time goes:
time: 791 us; the launch traced here: 776 us
  local copies, waits for them, and re-layouts  246 us (31%)
  blocking collectives  211 us (27%)
  waiting for transfers between devices  203 us (26%)
  matrix products  38.4 us (5%)
  other arithmetic  31.5 us (4%)
  starting transfers between devices  28 us (4%)
  between operations  14 us (2%)
    all_to_all x1, blocking collectives, body(): lax.all_to_all(rows_send, 'req', split_axis=0, concat_axis=0, tiled=True)  211 us
    unnamed x37, local copies, waits for them, and re-layouts  170 us
    all_gather x1, waiting for transfers between devices, body(): page_rows = lax.all_gather(prefix_cache, 'req', axis=1, tiled=True)  56.3 us
    all_to_all x1, waiting for transfers between devices, body(): lax.all_to_all(moved, 'req', split_axis=0, concat_axis=0, tiled=True)  55.5 us
    psum x1, waiting for transfers between devices, body(): residual = lax.psum((partial_value + placed).astype(jnp.bfloat16), 'tp')  43.8 us
    unnamed x4, waiting for transfers between devices  30.3 us
    reshape x1, local copies, waits for them, and re-layouts, body(): chosen.reshape(requests, span_rows // block_rows, block_rows, 2, kv_local...  17.5 us
  transfers between devices with their start and end apart: 7, of which 6 were waited for; matrix products, arithmetic and copies ran while one was open for 12% of the time, Pallas kernels for 0%

commit v1 on v0

--- a/solution.py
+++ b/solution.py
@@ -30,29 +30,6 @@
         [front_half * cosine - back_half * sine_part, back_half * cosine + front_half * sine_part],
         axis=-1,
     )
-
-
-def absorb_block(softmax_state, query_groups, block_keys, block_values, allowed):
-    run_max, run_sum, run_acc = softmax_state
-    score_matrix = (
-        jnp.einsum(
-            "rskgd,rbkd->rskgb", query_groups, block_keys, preferred_element_type=jnp.float32
-        )
-        * logit_scale
-    )
-    if allowed is not None:
-        score_matrix = jnp.where(allowed, score_matrix, masked_score)
-    new_max = jnp.maximum(run_max, jnp.max(score_matrix, axis=-1))
-    rescale = jnp.exp(run_max - new_max)
-    weights = jnp.exp(score_matrix - new_max[..., None])
-    new_sum = run_sum * rescale + jnp.sum(weights, axis=-1)
-    new_acc = run_acc * rescale[..., None] + jnp.einsum(
-        "rskgb,rbkd->rskgd",
-        weights.astype(jnp.bfloat16),
-        block_values,
-        preferred_element_type=jnp.float32,
-    )
-    return (new_max, new_sum, new_acc)
 
 
 def body(
@@ -89,35 +66,55 @@
     fresh_keys = fresh_keys.reshape(requests, suffix, kv_local, HD)
     fresh_values = key_values[:, 1].reshape(requests, suffix, kv_local, HD)
     sink_values = sink_logits.reshape(kv_local, per_group)
-    state_shape = (requests, suffix, kv_local, per_group)
-    start_state = (
-        jnp.broadcast_to(sink_values[None, None], state_shape),
-        jnp.ones(state_shape, jnp.float32),
-        jnp.zeros(state_shape + (HD,), jnp.float32),
-    )
     page_rows = lax.all_gather(prefix_cache, "req", axis=1, tiled=True)
     span_rows = page_rows.shape[1]
-    block_rows = 512
-    chosen = page_rows[groups]
-    stacked = chosen.reshape(requests, span_rows // block_rows, block_rows, 2, kv_local, HD)
-
-    def absorb_one(inner_state, block_index):
-        block_pair = lax.dynamic_index_in_dim(stacked, block_index, 1, keepdims=False)
-        return (
-            absorb_block(inner_state, query_groups, block_pair[:, :, 0], block_pair[:, :, 1], None),
-            None,
+    pages_t = page_rows.reshape(page_rows.shape[0], span_rows, 2, kv_local, HD).transpose(
+        0, 2, 3, 1, 4
+    )
+    chosen = pages_t[groups]
+    prefix_keys = chosen[:, 0]
+    prefix_values = chosen[:, 1]
+    prefix_scores = (
+        jnp.einsum(
+            "rskgd,rkbd->rskgb", query_groups, prefix_keys, preferred_element_type=jnp.float32
         )
-
-    final_state, _ = lax.scan(absorb_one, start_state, jnp.arange(span_rows // block_rows))
+        * logit_scale
+    )
     local_pos = jnp.arange(suffix, dtype=jnp.int32)
     causal = local_pos[None, :] <= local_pos[:, None]
     within = local_pos[None, None, :] < lengths[:, None, None]
     allowed = (causal[None] & within)[:, :, None, None, :]
-    run_max, run_sum, run_acc = absorb_block(
-        final_state, query_groups, fresh_keys, fresh_values, allowed
+    suffix_scores = (
+        jnp.einsum(
+            "rskgd,rbkd->rskgb", query_groups, fresh_keys, preferred_element_type=jnp.float32
+        )
+        * logit_scale
+    )
+    suffix_scores = jnp.where(allowed, suffix_scores, masked_score)
+    top_score = jnp.maximum(
+        jnp.maximum(jnp.max(prefix_scores, axis=-1), jnp.max(suffix_scores, axis=-1)),
+        sink_values[None, None],
+    )
+    prefix_weights = jnp.exp(prefix_scores - top_score[..., None])
+    suffix_weights = jnp.exp(suffix_scores - top_score[..., None])
+    totals = (
+        jnp.sum(prefix_weights, axis=-1)
+        + jnp.sum(suffix_weights, axis=-1)
+        + jnp.exp(sink_values[None, None] - top_score)
+    )
+    value_acc = jnp.einsum(
+        "rskgb,rkbd->rskgd",
+        prefix_weights.astype(jnp.bfloat16),
+        prefix_values,
+        preferred_element_type=jnp.float32,
+    ) + jnp.einsum(
+        "rskgb,rbkd->rskgd",
+        suffix_weights.astype(jnp.bfloat16),
+        fresh_values,
+        preferred_element_type=jnp.float32,
     )
     attention = (
-        (run_acc / run_sum[..., None]).reshape(tokens, local_heads * HD).astype(jnp.bfloat16)
+        (value_acc / totals[..., None]).reshape(tokens, local_heads * HD).astype(jnp.bfloat16)
     )
     partial_value = jnp.dot(attention, output_weight, preferred_element_type=jnp.float32)
     tp_index = lax.axis_index("tp")
@@ -174,24 +171,30 @@
     rows_in = lax.all_to_all(rows_send, "req", split_axis=0, concat_axis=0, tiled=True)
     arrived_weight = lax.all_to_all(weight_send, "req", split_axis=0, concat_axis=0, tiled=True)
     arrived_token = lax.all_to_all(token_send, "req", split_axis=0, concat_axis=0, tiled=True)
-    rows_float = rows_in.astype(jnp.float32)
+    n_tp = lax.axis_size("tp")
+    rows_flat = rows_in.reshape(-1, D)
+    rows_float = rows_flat.astype(jnp.float32)
     row_scale = lax.rsqrt(jnp.mean(rows_float * rows_float, axis=-1, keepdims=True) + norm_eps)
     normed = (rows_float * row_scale * norm_gain).astype(jnp.bfloat16)
     gate_and_up = jnp.einsum(
-        "njcd,jdgf->njcgf", normed, gate_up, preferred_element_type=jnp.float32
-    )
-    hidden = (jax.nn.silu(gate_and_up[..., 0, :]) * gate_and_up[..., 1, :]).astype(jnp.bfloat16)
+        "nd,dgf->ngf", normed, gate_up[0], preferred_element_type=jnp.float32
+    )
+    hidden = (jax.nn.silu(gate_and_up[:, 0, :]) * gate_and_up[:, 1, :]).astype(jnp.bfloat16)
+    down_chunks = expert_down[0].reshape(expert_down.shape[1], n_tp, quarter_cols)
     partial_out = jnp.einsum(
-        "njcf,jfd->njcd", hidden, expert_down, preferred_element_type=jnp.float32
+        "nf,ftd->tnd", hidden, down_chunks, preferred_element_type=jnp.float32
     )
     value_total = lax.psum_scatter(
-        partial_out.astype(jnp.bfloat16), "tp", scatter_dimension=3, tiled=True
-    ).astype(jnp.float32)
-    own_rows = lax.dynamic_slice_in_dim(rows_float, tp_index * quarter_cols, quarter_cols, 3)
+        partial_out.astype(jnp.bfloat16), "tp", scatter_dimension=0, tiled=True
+    )[0].astype(jnp.float32)
+    own_rows = lax.dynamic_slice_in_dim(rows_flat, tp_index * quarter_cols, quarter_cols, 1).astype(
+        jnp.float32
+    )
+    slab_rows = rows_in.shape[0] * rows_in.shape[2]
     result = (
-        arrived_weight.astype(jnp.float32)[..., None]
-        * (value_total + first_copy[None, :, None, None] * own_rows)
-    ).astype(jnp.bfloat16)
+        arrived_weight.reshape(slab_rows).astype(jnp.float32)[:, None]
+        * (value_total + first_copy[0] * own_rows)
+    ).astype(jnp.bfloat16).reshape(rows_in.shape[0], 1, rows_in.shape[2], quarter_cols)
     moved = result[inverse]
     moved_token = arrived_token[inverse]
     returned = lax.all_to_all(moved, "req", split_axis=0, concat_axis=0, tiled=True)

time: 791 us -> 590 us (0.75)
  waiting for transfers between devices: 203 us -> 418 us
  blocking collectives: 211 us -> 0 us
  local copies, waits for them, and re-layouts: 246 us -> 49.5 us
  starting transfers between devices: 28 us -> 38.7 us
    all_to_all x1 -> x0, blocking collectives: 211 us -> none  [body(): lax.all_to_all(rows_send, 'req', split_axis=0, concat_axis=0, tiled=True)]
    all_to_all x0 -> x1, waiting for transfers between devices: none -> 197 us  [body(): lax.all_to_all(rows_send, 'req', split_axis=0, concat_axis=0, tiled=True)]
    unnamed x37 -> x22, local copies, waits for them, and re-layouts: 170 us -> 8 us
    reduce_scatter x0 -> x1, waiting for transfers between devices: none -> 35.7 us  [body(): lax.psum_scatter(partial_out.astype(jnp.bfloat16), 'tp', scatter_dimensio...]
    unnamed x4 -> x3, waiting for transfers between devices: 30.3 us -> 0.05 us
    reshape x1 -> x0, local copies, waits for them, and re-layouts: 17.5 us -> none  [body(): chosen.reshape(requests, span_rows // block_rows, block_rows, 2, kv_local...]
    all_gather x1, waiting for transfers between devices: 56.3 us -> 70.3 us  [body(): page_rows = lax.all_gather(prefix_cache, 'req', axis=1, tiled=True)]
    all_to_all x0 -> x1, starting transfers between devices: none -> 10.7 us  [body(): lax.all_to_all(rows_send, 'req', split_axis=0, concat_axis=0, tiled=True)]
  transfers between devices with their start and end apart: 7 -> 8, of which waited for: 6 -> 7; matrix products, arithmetic and copies ran while one was open for 12% -> 7% of each run, Pallas kernels for 0% -> 0%
where the time goes in v1:
time: 590 us; the launch traced here: 581 us
  waiting for transfers between devices  418 us (71%)
  local copies, waits for them, and re-layouts  49.5 us (8%)
  starting transfers between devices  38.7 us (7%)
  matrix products  32.2 us (5%)
  other arithmetic  28.1 us (5%)
  between operations  13.8 us (2%)
    all_to_all x1, waiting for transfers between devices, body(): lax.all_to_all(rows_send, 'req', split_axis=0, concat_axis=0, tiled=True)  197 us
    all_gather x1, waiting for transfers between devices, body(): page_rows = lax.all_gather(prefix_cache, 'req', axis=1, tiled=True)  70.3 us
    all_to_all x1, waiting for transfers between devices, body(): lax.all_to_all(moved, 'req', split_axis=0, concat_axis=0, tiled=True)  55.5 us
    psum x1, waiting for transfers between devices, body(): residual = lax.psum((partial_value + placed).astype(jnp.bfloat16), 'tp')  43.1 us
    reduce_scatter x1, waiting for transfers between devices, body(): lax.psum_scatter(partial_out.astype(jnp.bfloat16), 'tp', scatter_dimensio...  35.7 us
  transfers between devices with their start and end apart: 8, of which 7 were waited for; matrix products, arithmetic and copies ran while one was open for 7% of the time, Pallas kernels for 0%

profile of v1, /device:TPU:2, one launch (start us, length us, event | category | flops | bytes accessed | tf_op | source)
XLA Modules:
  0.0 580.7 jit_solution(18267216493220123332)
XLA Ops:
  19.2 70.3 %all-gather.2.cloned.1.call-done = bf16[4,1024,2,128]{3,0,2,1:T(4,128)(2,1)} async-done(((bf16[4,16,2,128]{3,0,2,1:T(4,128)(2,1)}), bf16[4,1024,2,128]{3,0,2,1:T(4,128)(2,1)}) %all-gather.2.cloned.1.call-update) | async-done | bytes 2097168 | tf_op jit(solution)/shard_map/all_gather | solution.py:69
  89.5 3.0 copy.86
  95.2 3.1 bitcast_reduce_fusion
  103.6 4.4 fusion.52
  114.1 43.1 %all-reduce.3.cloned.1.call-done = bf16[128,2880]{0,1:T(8,128)(2,1)} async-done(((bf16[128,2880]{0,1:T(8,128)(2,1)}), bf16[128,2880]{0,1:T(8,128)(2,1)}) %all-reduce.3.cloned.1.call-update) | async-done | bytes 737296 | tf_op jit(solution)/shard_map/psum | solution.py:128
  158.8 8.0 %gather_fusion.4 = bf16[1536,2880]{1,0:T(8,128)(2,1)} fusion(bf16[129,2880]{1,0:T(8,128)(2,1)S(1)} %concatenate.27.clone, s32[2048]{0:T(1024)S(1)} %pad_clamp_fusion), kind=kCustom, calls=%fused_computation.4 | custom fusion | bytes 17700864 | tf_op jit(solution)/shard_map/gather | solution.py:161
  166.8 10.7 %all-to-all-start.3 = ((bf16[64,1,24,2880]{3,2,1,0:T(8,128)(2,1)}), bf16[64,1,24,2880]{3,2,1,0:T(8,128)(2,1)}, u32[]{:S(2)}, u32[]{:S(2)}) async-start(bf16[64,1,24,2880]{3,2,1,0:T(8,128)(2,1)} %bitcast.140), calls=%async_computation.3 | async-start | bytes 18087936 | tf_op jit(solution)/shard_map/all_to_all | solution.py:171
  177.6 3.4 copy.121
  180.9 196.9 %all-to-all-done.3 = bf16[64,1,24,2880]{3,2,1,0:T(8,128)(2,1)} async-done(((bf16[64,1,24,2880]{3,2,1,0:T(8,128)(2,1)}), bf16[64,1,24,2880]{3,2,1,0:T(8,128)(2,1)}, u32[]{:S(2)}, u32[]{:S(2)}) %all-to-all-start.3) | async-done | bytes 8847392 | tf_op jit(solution)/shard_map/all_to_all | solution.py:171
  377.8 5.4 fusion
  383.2 10.5 %fusion.2 = bf16[64,1,24,2880]{3,2,1,0:T(8,128)(2,1)} fusion(bf16[64,1,24,2880]{3,2,1,0:T(8,128)(2,1)} %all-to-all-done.3, f32[2880]{0:T(1024)S(1)} %copy-done.4, f32[64,24]{1,0:T(8,128)S(1)} %add_rsqrt_fusion), kind=kLoop, calls=%fused_computation.12 | loop fusion | flops 17694720 | bytes 17712384 | tf_op jit(solution)/shard_map/convert_element_type | solution.py:178
  393.8 10.9 %fusion.8 = f32[1536,2,360]{0,2,1:T(8,128)S(1)} fusion(bf16[1536,2880,1]{1,0,2:T(8,128)(2,1)} %bitcast.143, bf16[1,2880,2,360]{1,3,2,0:T(8,128)(2,1)} %param.26), kind=kOutput, calls=%fused_computation.22 | convolution fusion | flops 6370099200 | bytes 17418240 | tf_op jit(solution)/shard_map/nd,dgf->ngf/dot_general | solution.py:179
  404.7 7.4 %convert_bitcast_fusion = bf16[4,1536,720]{1,2,0:T(8,128)(2,1)} fusion(bf16[360,4,720]{0,2,1:T(8,128)(2,1)S(1)} %bitcast.145, f32[1536,2,360]{0,2,1:T(8,128)S(1)} %fusion.8), kind=kOutput, calls=%fused_computation.13 | convolution fusion | flops 3192791040 | bytes 15344640 | tf_op jit(solution)/shard_map/nf,ftd->tnd/dot_general | solution.py:184
  413.0 3.9 scatter_custom_fusion.1
  418.4 6.4 %all-to-all-start.2 = ((bf16[64,1,24]{2,1,0:T(2,128)(2,1)}), bf16[64,1,24]{2,1,0:T(2,128)(2,1)S(1)}, u32[]{:S(2)}, u32[]{:S(2)}) async-start(bf16[64,1,24]{2,1,0:T(2,128)(2,1)} %copy.84), calls=%async_computation.2 | async-start | bytes 65536 | tf_op jit(solution)/shard_map/all_to_all | solution.py:172
  424.9 8.5 %all-to-all-done.2 = bf16[64,1,24]{2,1,0:T(2,128)(2,1)S(1)} async-done(((bf16[64,1,24]{2,1,0:T(2,128)(2,1)}), bf16[64,1,24]{2,1,0:T(2,128)(2,1)S(1)}, u32[]{:S(2)}, u32[]{:S(2)}) %all-to-all-start.2) | async-done | bytes 3104 | tf_op jit(solution)/shard_map/all_to_all | solution.py:172
  433.4 5.5 all-to-all-start
  439.0 8.5 %all-to-all-done = s32[64,1,24]{2,1,0:T(1,128)S(1)} async-done(((s32[64,1,24]{2,1,0:T(1,128)}), s32[64,1,24]{2,1,0:T(1,128)S(1)}, u32[]{:S(2)}, u32[]{:S(2)}) %all-to-all-start) | async-done | bytes 6176 | tf_op jit(solution)/shard_map/all_to_all | solution.py:173
  448.7 5.5 all-to-all-start.1
  454.2 3.1 constant_dynamic-slice_fusion
  459.8 35.7 %reduce-scatter.2.cloned.1.call-done = bf16[1,1536,720]{1,2,0:T(8,128)(2,1)} async-done(((bf16[4,1536,720]{1,2,0:T(8,128)(2,1)}), bf16[1,1536,720]{1,2,0:T(8,128)(2,1)}) %reduce-scatter.2.cloned.1.call-update) | async-done | bytes 2211856 | tf_op jit(solution)/shard_map/reduce_scatter | solution.py:187
  495.5 4.5 fusion.7
  504.9 10.6 %all-to-all-start.4 = ((bf16[64,1,24,720]{3,2,1,0:T(8,128)(2,1)}), bf16[64,1,24,720]{3,2,1,0:T(8,128)(2,1)S(1)}, u32[]{:S(2)}, u32[]{:S(2)}) async-start(bf16[64,1,24,720]{3,2,1,0:T(8,128)(2,1)} %bitcast.50), calls=%async_computation.5 | async-start | bytes 4718592 | tf_op jit(solution)/shard_map/all_to_all | solution.py:200
  516.8 55.5 %all-to-all-done.4 = bf16[64,1,24,720]{3,2,1,0:T(8,128)(2,1)S(1)} async-done(((bf16[64,1,24,720]{3,2,1,0:T(8,128)(2,1)}), bf16[64,1,24,720]{3,2,1,0:T(8,128)(2,1)S(1)}, u32[]{:S(2)}, u32[]{:S(2)}) %all-to-all-start.4) | async-done | bytes 2211872 | tf_op jit(solution)/shard_map/all_to_all | solution.py:200
  (107 shorter events, 42.3 us)
Async XLA Ops:
  6.5 10.0 %copy-start.5 = (s32[8]{0:T(128)S(1)}, s32[8]{0:T(128)}, u32[]{:S(2)}) copy-start(s32[8]{0:T(128)} %param.20) | copy-start | bytes 100
  6.5 10.1 %copy-start.6 = (s32[8]{0:T(128)S(1)}, s32[8]{0:T(128)}, u32[]{:S(2)}) copy-start(s32[8]{0:T(128)} %param.19) | copy-start | bytes 100
  6.5 83.0 %all-gather.2.cloned.1.call-start = ((), (), s32[]{:S(2)}) async-start(), calls=%async_computation.6 | async-start | bytes 2129920 | tf_op jit(solution)/shard_map/all_gather | solution.py:69
  8.0 149.3 %all-reduce.3.cloned.1.call-start = ((), (), s32[]{:S(2)}) async-start(), calls=%async_computation.7 | async-start | bytes 1474560 | tf_op jit(solution)/shard_map/psum | solution.py:128
  95.2 3.2 copy-start
  100.3 1.9 copy-start.1
  103.6 4.4 copy-start.2
  166.8 211.0 %all-to-all-start.3 = ((bf16[64,1,24,2880]{3,2,1,0:T(8,128)(2,1)}), bf16[64,1,24,2880]{3,2,1,0:T(8,128)(2,1)}, u32[]{:S(2)}, u32[]{:S(2)}) async-start(bf16[64,1,24,2880]{3,2,1,0:T(8,128)(2,1)} %bitcast.140), calls=%async_computation.3 | async-start | bytes 18087936 | tf_op jit(solution)/shard_map/all_to_all | solution.py:171
  177.5 318.0 %reduce-scatter.2.cloned.1.call-start = ((), (), s32[]{:S(2)}) async-start(), calls=%async_computation.8 | async-start | bytes 11059200 | tf_op jit(solution)/shard_map/reduce_scatter | solution.py:187
  180.9 202.3 %copy-start.4 = (f32[2880]{0:T(1024)S(1)}, f32[2880]{0:T(1024)}, u32[]{:S(2)}) copy-start(f32[2880]{0:T(1024)} %param.24) | copy-start | bytes 34564
  412.0 0.7 copy-start.3
  412.0 12.7 %copy-start.7 = (s32[64]{0:T(128)S(1)}, s32[64]{0:T(128)}, u32[]{:S(2)}) copy-start(s32[64]{0:T(128)} %param.21) | copy-start | bytes 772
  418.4 15.0 %all-to-all-start.2 = ((bf16[64,1,24]{2,1,0:T(2,128)(2,1)}), bf16[64,1,24]{2,1,0:T(2,128)(2,1)S(1)}, u32[]{:S(2)}, u32[]{:S(2)}) async-start(bf16[64,1,24]{2,1,0:T(2,128)(2,1)} %copy.84), calls=%async_computation.2 | async-start | bytes 65536 | tf_op jit(solution)/shard_map/all_to_all | solution.py:172
  433.4 14.1 %all-to-all-start = ((s32[64,1,24]{2,1,0:T(1,128)}), s32[64,1,24]{2,1,0:T(1,128)S(1)}, u32[]{:S(2)}, u32[]{:S(2)}) async-start(s32[64,1,24]{2,1,0:T(1,128)} %bitcast.5), calls=%async_computation | async-start | bytes 65536 | tf_op jit(solution)/shard_map/all_to_all | solution.py:173
  448.7 56.2 %all-to-all-start.1 = ((s32[64,1,24]{2,1,0:T(1,128)}), s32[64,1,24]{2,1,0:T(1,128)S(1)}, u32[]{:S(2)}, u32[]{:S(2)}) async-start(s32[64,1,24]{2,1,0:T(1,128)} %bitcast.10), calls=%async_computation.1 | async-start | bytes 65536 | tf_op jit(solution)/shard_map/all_to_all | solution.py:201
  504.9 67.4 %all-to-all-start.4 = ((bf16[64,1,24,720]{3,2,1,0:T(8,128)(2,1)}), bf16[64,1,24,720]{3,2,1,0:T(8,128)(2,1)S(1)}, u32[]{:S(2)}, u32[]{:S(2)}) async-start(bf16[64,1,24,720]{3,2,1,0:T(8,128)(2,1)} %bitcast.50), calls=%async_computation.5 | async-start | bytes 4718592 | tf_op jit(solution)/shard_map/all_to_all | solution.py:200
Sparse Core Ops, SparseCore 0:
  10.1 79.3 all-gather.1
  109.2 47.9 all-reduce.2
  412.2 83.2 reduce-scatter.1

commit v2 on v1

v2 whole, which is shorter than its diff:
```python
import jax
import jax.numpy as jnp
from jax import lax
from jax.sharding import Mesh, PartitionSpec as P

D = 2880
HD = 64
EXPERTS = 32
TOPK = 4
PREFIX = 1024
CAP = 24


theta_base = 150000.0
norm_eps = 1e-05
logit_scale = 0.125
masked_score = -1e30


def rotate(values, positions):
    middle = values.shape[-1] // 2
    lane_index = jnp.arange(middle, dtype=jnp.int32).astype(jnp.float32)
    inverse_freq = theta_base ** (-2.0 * lane_index / values.shape[-1])
    angles = positions.astype(jnp.float32)[:, None] * inverse_freq[None, :]
    cosine = jnp.cos(angles)[:, None, :]
    sine_part = jnp.sin(angles)[:, None, :]
    front_half = values[..., :middle]
    back_half = values[..., middle:]
    return jnp.concatenate(
        [front_half * cosine - back_half * sine_part, back_half * cosine + front_half * sine_part],
        axis=-1,
    )


def body(
    layer_in,
    queries,
    key_values,
    prefix_cache,
    sink_logits,
    lengths,
    groups,
    batch_home,
    expert_ids,
    router_logits,
    norm_gain,
    output_weight,
    gate_up,
    expert_down,
):
    tokens = queries.shape[0]
    requests = lengths.shape[0]
    suffix = tokens // requests
    local_heads = sink_logits.shape[0]
    kv_local = key_values.shape[2] // HD
    per_group = local_heads // kv_local
    slot_index = jnp.tile(jnp.arange(suffix, dtype=jnp.int32), requests)
    positions = PREFIX + slot_index
    rotated_queries = rotate(
        queries.reshape(tokens, local_heads, HD).astype(jnp.float32), positions
    ).astype(jnp.bfloat16)
    query_groups = rotated_queries.reshape(requests, suffix, kv_local, per_group, HD)
    fresh_keys = rotate(
        key_values[:, 0].reshape(tokens, kv_local, HD).astype(jnp.float32), positions
    ).astype(jnp.bfloat16)
    fresh_keys = fresh_keys.reshape(requests, suffix, kv_local, HD)
    fresh_values = key_values[:, 1].reshape(requests, suffix, kv_local, HD)
    sink_values = sink_logits.reshape(kv_local, per_group)
    page_rows = lax.all_gather(prefix_cache, ("chip", "core"), axis=1, tiled=True)
    span_rows = page_rows.shape[1]
    pages_t = page_rows.reshape(page_rows.shape[0], span_rows, 2, kv_local, HD).transpose(
        0, 2, 3, 1, 4
    )
    chosen = pages_t[groups]
    prefix_keys = chosen[:, 0]
    prefix_values = chosen[:, 1]
    prefix_scores = (
        jnp.einsum(
            "rskgd,rkbd->rskgb", query_groups, prefix_keys, preferred_element_type=jnp.float32
        )
        * logit_scale
    )
    local_pos = jnp.arange(suffix, dtype=jnp.int32)
    causal = local_pos[None, :] <= local_pos[:, None]
    within = local_pos[None, None, :] < lengths[:, None, None]
    allowed = (causal[None] & within)[:, :, None, None, :]
    suffix_scores = (
        jnp.einsum(
            "rskgd,rbkd->rskgb", query_groups, fresh_keys, preferred_element_type=jnp.float32
        )
        * logit_scale
    )
    suffix_scores = jnp.where(allowed, suffix_scores, masked_score)
    top_score = jnp.maximum(
        jnp.maximum(jnp.max(prefix_scores, axis=-1), jnp.max(suffix_scores, axis=-1)),
        sink_values[None, None],
    )
    prefix_weights = jnp.exp(prefix_scores - top_score[..., None])
    suffix_weights = jnp.exp(suffix_scores - top_score[..., None])
    totals = (
        jnp.sum(prefix_weights, axis=-1)
        + jnp.sum(suffix_weights, axis=-1)
        + jnp.exp(sink_values[None, None] - top_score)
    )
    value_acc = jnp.einsum(
        "rskgb,rkbd->rskgd",
        prefix_weights.astype(jnp.bfloat16),
        prefix_values,
        preferred_element_type=jnp.float32,
    ) + jnp.einsum(
        "rskgb,rbkd->rskgd",
        suffix_weights.astype(jnp.bfloat16),
        fresh_values,
        preferred_element_type=jnp.float32,
    )
    attention = (
        (value_acc / totals[..., None]).reshape(tokens, local_heads * HD).astype(jnp.bfloat16)
    )
    n_tp = lax.axis_size("tp")
    tp_index = lax.axis_index("tp")
    core = lax.axis_index("core")
    n_chips = lax.axis_size("chip")
    quarter_cols = D // n_tp
    out_chunks = output_weight.reshape(output_weight.shape[0], n_tp, quarter_cols)
    partial_value = jnp.einsum(
        "nh,htd->tnd", attention, out_chunks, preferred_element_type=jnp.float32
    )
    own_chunk = (jnp.arange(n_tp, dtype=jnp.int32) == tp_index)[:, None, None]
    placed = jnp.where(own_chunk, layer_in.astype(jnp.float32)[None], 0.0)
    residual = lax.psum_scatter(partial_value + placed, "tp", scatter_dimension=0, tiled=True)[
        0
    ].astype(jnp.bfloat16)
    live_rows = slot_index < jnp.repeat(lengths, suffix)
    pair_weight = jnp.where(live_rows[:, None], jax.nn.softmax(router_logits, axis=-1), 0.0).astype(
        jnp.bfloat16
    )
    flat_ids = expert_ids.reshape(-1)
    onehot = (flat_ids[:, None] == jnp.arange(EXPERTS, dtype=jnp.int32)[None, :]).astype(jnp.int32)
    before = jnp.cumsum(onehot, axis=0) - onehot
    rank_in = jnp.sum(before * onehot, axis=1)
    flat_slot = flat_ids * CAP + rank_in
    pair_token = jnp.arange(tokens * TOPK, dtype=jnp.int32) // TOPK
    token_table = (
        jnp.full((EXPERTS * CAP,), tokens, dtype=jnp.int32)
        .at[flat_slot]
        .set(pair_token)
        .reshape(EXPERTS, CAP)
    )
    weight_table = (
        jnp.zeros((EXPERTS * CAP,), jnp.float32)
        .at[flat_slot]
        .set(pair_weight.reshape(-1).astype(jnp.float32))
        .reshape(EXPERTS, CAP)
    )
    meta_send = jnp.stack([token_table.astype(jnp.float32), weight_table], axis=-1)
    padded = jnp.concatenate([residual, jnp.zeros((1, quarter_cols), jnp.bfloat16)], axis=0)
    rows_send = padded[token_table]
    partner = [(0, 1), (1, 0)]
    rows_own = lax.all_to_all(rows_send, "chip", 0, 0, tiled=True)
    meta_own = lax.all_to_all(meta_send, "chip", 0, 0, tiled=True)
    rows_gathered = lax.all_gather(rows_own, "tp", axis=0, tiled=False)
    rows_other = lax.ppermute(rows_gathered, "core", partner)
    meta_other = lax.ppermute(meta_own, "core", partner)
    all_rows = jnp.concatenate([rows_gathered, rows_other], axis=1)
    all_meta = jnp.concatenate([meta_own, meta_other], axis=0)
    slab_rows = all_rows.shape[1] * all_rows.shape[2]
    rows_q = all_rows.reshape(n_tp, slab_rows, quarter_cols)
    rows_float = rows_q.astype(jnp.float32)
    row_scale = lax.rsqrt(
        jnp.mean(rows_float * rows_float, axis=(0, 2), keepdims=True) + norm_eps
    )
    gain_q = norm_gain.reshape(n_tp, 1, quarter_cols)
    normed = (rows_float * row_scale * gain_q).astype(jnp.bfloat16)
    gate_q = gate_up[0].reshape(n_tp, quarter_cols, 2, gate_up.shape[3])
    gate_and_up = jnp.einsum(
        "tnd,tdgf->ngf", normed, gate_q, preferred_element_type=jnp.float32
    )
    hidden = (jax.nn.silu(gate_and_up[:, 0, :]) * gate_and_up[:, 1, :]).astype(jnp.bfloat16)
    down_chunks = expert_down[0].reshape(expert_down.shape[1], n_tp, quarter_cols)
    partial_out = jnp.einsum(
        "nf,ftd->tnd", hidden, down_chunks, preferred_element_type=jnp.float32
    )
    value_total = lax.psum_scatter(
        partial_out.astype(jnp.bfloat16), "tp", scatter_dimension=0, tiled=True
    )[0].astype(jnp.float32)
    own_rows = lax.dynamic_index_in_dim(rows_q, tp_index, 0, keepdims=False).astype(jnp.float32)
    first_copy = (core == 0).astype(jnp.float32)
    row_weight = all_meta[..., 1].reshape(slab_rows)
    result = (row_weight[:, None] * (value_total + first_copy * own_rows)).astype(jnp.bfloat16)
    result = result.reshape(all_meta.shape[0], all_meta.shape[1], quarter_cols)
    row_token = all_meta[..., 0]
    devices_req = 2 * n_chips
    device_range = jnp.arange(devices_req, dtype=jnp.int32)
    inverse = jnp.sum(
        device_range[:, None] * (batch_home[:, None] == device_range[None, :]).astype(jnp.int32),
        axis=0,
    )
    home_chip = jnp.arange(n_chips, dtype=jnp.int32)
    keep_batch = inverse[2 * home_chip + core]
    send_batch = inverse[2 * home_chip + 1 - core]

    def local_index(batch):
        return jnp.where(batch % 2 == core, 0, n_chips) + batch // 2

    keep = result[local_index(keep_batch)]
    sent = result[local_index(send_batch)]
    received = lax.ppermute(sent, "core", partner)
    summed = (keep.astype(jnp.float32) + received.astype(jnp.float32)).astype(jnp.bfloat16)
    keep_token = row_token[local_index(keep_batch)]
    returned = lax.all_to_all(summed, "chip", 0, 0, tiled=True)
    returned_token = lax.all_to_all(keep_token, "chip", 0, 0, tiled=True)
    flat_rows = returned.reshape(-1, quarter_cols)
    flat_token = returned_token.reshape(-1).astype(jnp.int32)
    selector = (jnp.arange(tokens, dtype=jnp.int32)[:, None] == flat_token[None, :]).astype(
        jnp.bfloat16
    )
    return jnp.dot(selector, flat_rows, preferred_element_type=jnp.float32).astype(jnp.bfloat16)


def solution(mesh):
    req = ("chip", "core")
    n_req, n_tp = mesh.devices.shape
    split_mesh = Mesh(mesh.devices.reshape(n_req // 2, 2, n_tp), ("chip", "core", "tp"))
    placed = (
        P(req, "tp"),
        P(req, "tp"),
        P(req, None, "tp"),
        P(None, req, None, "tp"),
        P("tp"),
        P(req),
        P(req),
        P(),
        P(req, None),
        P(req, None),
        P(),
        P("tp", None),
        P(req, None, None, "tp"),
        P(req, "tp", None),
    )
    return jax.shard_map(
        body, mesh=split_mesh, in_specs=placed, out_specs=P(req, "tp"), check_vma=False
    )
```

time: 590 us -> 442 us (0.75); the launches traced: 581 us -> 441 us
  waiting for transfers between devices: 418 us -> 241 us
  blocking collectives: 0 us -> 58.4 us
  starting transfers between devices: 38.7 us -> 15.4 us
    all_to_all x5 -> x2, waiting for transfers between devices: 269 us -> 34.9 us  [the longest x1 29.8 us: body(): returned = lax.all_to_all(summed, 'chip', 0, 0, tiled=True)]
    all_to_all x0 -> x2, blocking collectives: none -> 58.4 us  [the longest x1 39.8 us: body(): rows_own = lax.all_to_all(rows_send, 'chip', 0, 0, tiled=True)]
    all_gather x1 -> x2, waiting for transfers between devices: 70.3 us -> 125 us  [the longest x1 73.9 us: body(): lax.all_gather(prefix_cache, ('chip', 'core'), axis=1, tiled=True)]
    psum x1 -> x0, waiting for transfers between devices: 43.1 us -> none  [body(): residual = lax.psum((partial_value + placed).astype(jnp.bfloat16), 'tp')]
    reduce_scatter x1, waiting for transfers between devices: 35.7 us -> 59.9 us  [body(): lax.psum_scatter(partial_out.astype(jnp.bfloat16), 'tp', scatter_dimensio...]
    all_to_all x5 -> x2, starting transfers between devices: 38.6 us -> 15.2 us  [the longest x1 10.2 us: body(): returned_token = lax.all_to_all(keep_token, 'chip', 0, 0, tiled=True)]
    reduce_scatter x0 -> x1, waiting for transfers between devices: none -> 20.7 us  [body(): lax.psum_scatter(partial_value + placed, 'tp', scatter_dimension=0, tiled...]
    another operation x5 -> x8, local copies, waits for them, and re-layouts: 1.11 us -> 12.3 us  [the longest x1 11.1 us: body(): gate_q = gate_up[0].reshape(n_tp, quarter_cols, 2, gate_up.shape[3])]
  transfers between devices with their start and end apart: 8 -> 9, of which waited for: 7 -> 7; matrix products, arithmetic and copies ran while one was open for 7% -> 9% of each run, Pallas kernels for 0% -> 0%
where the time goes in v2:
time: 442 us; the launch traced here: 441 us
  waiting for transfers between devices  241 us (55%)
  blocking collectives  58.4 us (13%)
  local copies, waits for them, and re-layouts  51.3 us (12%)
  matrix products  33.8 us (8%)
  other arithmetic  27.2 us (6%)
  starting transfers between devices  15.4 us (3%)
  between operations  13.7 us (3%)
    all_gather x1, waiting for transfers between devices, body(): lax.all_gather(prefix_cache, ('chip', 'core'), axis=1, tiled=True)  73.9 us
    reduce_scatter x1, waiting for transfers between devices, body(): lax.psum_scatter(partial_out.astype(jnp.bfloat16), 'tp', scatter_dimensio...  59.9 us
    all_gather x1, waiting for transfers between devices, body(): rows_gathered = lax.all_gather(rows_own, 'tp', axis=0, tiled=False)  50.8 us
    all_to_all x1, blocking collectives, body(): rows_own = lax.all_to_all(rows_send, 'chip', 0, 0, tiled=True)  39.8 us
    all_to_all x1, waiting for transfers between devices, body(): returned = lax.all_to_all(summed, 'chip', 0, 0, tiled=True)  29.8 us
    reduce_scatter x1, waiting for transfers between devices, body(): lax.psum_scatter(partial_value + placed, 'tp', scatter_dimension=0, tiled...  20.7 us
    all_to_all x1, blocking collectives, body(): meta_own = lax.all_to_all(meta_send, 'chip', 0, 0, tiled=True)  18.6 us
    dot_general x1, matrix products, body(): jnp.einsum('tnd,tdgf->ngf', normed, gate_q, preferred_element_type=jnp.fl...  11.3 us
  transfers between devices with their start and end apart: 9, of which 7 were waited for; matrix products, arithmetic and copies ran while one was open for 9% of the time, Pallas kernels for 0%

profile of v2, /device:TPU:2, one launch (start us, length us, event | category | flops | bytes accessed | tf_op | source)
XLA Modules:
  0.0 441.3 jit_solution(1842933867502077427)
XLA Ops:
  12.6 3.0 fusion.62
  15.6 73.9 %all-gather.4.cloned.1.call-done = bf16[4,1024,2,128]{3,0,2,1:T(4,128)(2,1)} async-done(((bf16[4,16,2,128]{3,0,2,1:T(4,128)(2,1)}), bf16[4,1024,2,128]{3,0,2,1:T(4,128)(2,1)}) %all-gather.4.cloned.1.call-update) | async-done | bytes 2097168 | tf_op jit(solution)/shard_map/all_gather | solution.py:69
  89.5 3.0 copy.90
  92.5 2.7 gather_fusion.2
  95.2 3.0 bitcast_reduce_fusion
  103.8 5.5 %bitcast_add_fusion = f32[4,128,720]{1,2,0:T(8,128)} fusion(bf16[128,1024,1]{1,0,2:T(8,128)(2,1)S(1)} %reshape.595, bf16[1024,4,720]{0,2,1:T(8,128)(2,1)} %bitcast.172, f32[128,720]{0,1:T(8,128)S(1)} %convert_element_type.205, pred[4]{0:T(512)(128)(4,1)S(1)} %iota_compare_fusion.7), kind=kOutput, calls=%fused_computation.35 | convolution fusion | flops 755712000 | bytes 8003588 | tf_op jit(solution)/shard_map/nh,htd->tnd/dot_general | solution.py:125
  115.1 20.7 %reduce-scatter.3.cloned.1.call-done = f32[1,128,720]{1,2,0:T(8,128)} async-done(((f32[4,128,720]{1,2,0:T(8,128)}), f32[1,128,720]{1,2,0:T(8,128)}) %reduce-scatter.3.cloned.1.call-update) | async-done | bytes 368656 | tf_op jit(solution)/shard_map/reduce_scatter | solution.py:130
  137.0 2.8 gather_fusion.3
  139.7 39.8 %all_to_all.24 = bf16[32,24,720]{2,1,0:T(8,128)(2,1)} all-to-all(bf16[32,24,720]{2,1,0:T(8,128)(2,1)S(1)} %bitcast.174), channel_id=1, replica_groups=mesh['chip'=32,'core'=2,'tp'=4] {'chip'}, dimensions={0} | all-to-all | bytes 2211840 | tf_op jit(solution)/shard_map/all_to_all | solution.py:159
  179.7 50.8 %all-gather.6.cloned.1.call-done = bf16[128,24,720]{2,1,0:T(8,128)(2,1)} async-done(((bf16[32,24,720]{2,1,0:T(8,128)(2,1)}), bf16[128,24,720]{2,1,0:T(8,128)(2,1)}) %all-gather.6.cloned.1.call-update) | async-done | bytes 4423696 | tf_op jit(solution)/shard_map/all_gather | solution.py:161
  230.4 11.1 %reshape_squeeze.11 = bf16[4,720,2,360]{1,0,3,2:T(4,128)(2,1)} reshape(bf16[1,2880,2,360]{1,3,2,0:T(8,128)(2,1)} %param.26) | data formatting | bytes 8294400 | tf_op jit(solution)/shard_map/reshape;squeeze | solution.py:174
  241.6 3.4 copy.125
  245.0 5.9 %multiply_reduce_fusion = f32[64,24]{1,0:T(8,128)S(1)} fusion(bf16[4,32,24,720]{3,2,1,0:T(8,128)(2,1)} %collective-permute-done.1, bf16[4,32,24,720]{3,2,1,0:T(8,128)(2,1)} %bitcast.168), kind=kLoop, calls=%fused_computation.10 | loop fusion | flops 17693184 | bytes 8853504 | tf_op jit(solution)/shard_map/reduce_sum | solution.py:170
  251.0 4.6 %pad_maximum_fusion = bf16[4,64,24,720]{3,2,1,0:T(8,128)(2,1)S(1)} fusion(bf16[4,32,24,720]{3,2,1,0:T(8,128)(2,1)} %collective-permute-done.1, bf16[4,32,24,720]{3,2,1,0:T(8,128)(2,1)} %bitcast.169), kind=kLoop, calls=%fused_computation.13 | loop fusion | flops 4423680 | bytes 17694720 | tf_op jit(solution)/shard_map/concatenate | solution.py:164
  255.6 11.3 %fusion.13 = f32[1536,2,360]{0,2,1:T(8,128)S(1)} fusion(bf16[4,720,2,360]{1,0,3,2:T(4,128)(2,1)} %reshape_squeeze.11, bf16[4,1536,720]{2,1,0:T(8,128)(2,1)S(1)} %bitcast.170, f32[4,720]{1,0:T(4,128)S(1)} %mul.281, f32[1536]{0:T(1024)S(1)} %rsqrt.12), kind=kOutput, calls=%fused_computation.28 | convolution fusion | flops 6387793920 | bytes 17435904 | tf_op jit(solution)/shard_map/tnd,tdgf->ngf/dot_general | solution.py:175
  266.9 7.4 %convert_bitcast_fusion = bf16[4,1536,720]{1,2,0:T(8,128)(2,1)} fusion(bf16[360,4,720]{0,2,1:T(8,128)(2,1)S(1)} %bitcast.175, f32[1536,2,360]{0,2,1:T(8,128)S(1)} %fusion.13), kind=kOutput, calls=%fused_computation.16 | convolution fusion | flops 3192791040 | bytes 15344640 | tf_op jit(solution)/shard_map/nf,ftd->tnd/dot_general | solution.py:180
  277.9 18.6 %all_to_all.25 = f32[32,24,2]{1,2,0:T(2,128)S(1)} all-to-all(f32[32,24,2]{1,2,0:T(2,128)S(1)} %copy.85), channel_id=1, replica_groups=mesh['chip'=32,'core'=2,'tp'=4] {'chip'}, dimensions={0} | all-to-all | bytes 12288 | tf_op jit(solution)/shard_map/all_to_all | solution.py:160
  302.0 59.9 %reduce-scatter.5.cloned.1.call-done = bf16[1,1536,720]{1,2,0:T(8,128)(2,1)} async-done(((bf16[4,1536,720]{1,2,0:T(8,128)(2,1)}), bf16[1,1536,720]{1,2,0:T(8,128)(2,1)}) %reduce-scatter.5.cloned.1.call-update) | async-done | bytes 2211856 | tf_op jit(solution)/shard_map/reduce_scatter | solution.py:183
  361.9 5.1 %multiply_add_fusion = f32[1,1536,720]{1,2,0:T(8,128)} fusion(bf16[1,1536,720]{1,2,0:T(8,128)(2,1)} %copy.129, bf16[1,1536,720]{1,2,0:T(8,128)(2,1)} %reduce-scatter.5.cloned.1.call-done, f32[]{:T(128)S(6)} %convert_element_type.216), kind=kLoop, calls=%fused_computation.24 | loop fusion | flops 4423680 | bytes 8847364 | tf_op jit(solution)/shard_map/add | solution.py:189
  367.0 5.9 %copy.111 = f32[1,1536,720]{2,1,0:T(8,128)} copy(f32[1,1536,720]{1,2,0:T(8,128)} %multiply_add_fusion) | data formatting | bytes 8847360 | tf_op jit(solution)/shard_map/add | solution.py:189
  379.2 10.2 %all-to-all-start.1 = ((f32[32,1,24]{2,1,0:T(1,128)}), f32[32,1,24]{2,1,0:T(1,128)}, u32[]{:S(2)}, u32[]{:S(2)}) async-start(f32[32,1,24]{2,1,0:T(1,128)} %bitcast.8), calls=%async_computation.1 | async-start | bytes 32768 | tf_op jit(solution)/shard_map/all_to_all | solution.py:211
  392.7 5.1 %all-to-all-done.1 = f32[32,1,24]{2,1,0:T(1,128)} async-done(((f32[32,1,24]{2,1,0:T(1,128)}), f32[32,1,24]{2,1,0:T(1,128)}, u32[]{:S(2)}, u32[]{:S(2)}) %all-to-all-start.1) | async-done | bytes 3104 | tf_op jit(solution)/shard_map/all_to_all | solution.py:211
  397.8 5.0 %all-to-all-start.3 = ((bf16[32,24,720]{2,1,0:T(8,128)(2,1)}), bf16[32,24,720]{2,1,0:T(8,128)(2,1)S(1)}, u32[]{:S(2)}, u32[]{:S(2)}) async-start(bf16[32,24,720]{2,1,0:T(8,128)(2,1)} %add_convert_fusion), calls=%async_computation.5 | async-start | bytes 2359296 | tf_op jit(solution)/shard_map/all_to_all | solution.py:210
  403.7 29.8 %all-to-all-done.3 = bf16[32,24,720]{2,1,0:T(8,128)(2,1)S(1)} async-done(((bf16[32,24,720]{2,1,0:T(8,128)(2,1)}), bf16[32,24,720]{2,1,0:T(8,128)(2,1)S(1)}, u32[]{:S(2)}, u32[]{:S(2)}) %all-to-all-start.3) | async-done | bytes 1105952 | tf_op jit(solution)/shard_map/all_to_all | solution.py:210
  (135 shorter events, 39.0 us)
Async XLA Ops:
  6.5 4.3 copy-start.4
  6.5 4.9 %copy-start.10 = (f32[16]{0:T(128)S(1)}, f32[16]{0:T(128)}, u32[]{:S(2)}) copy-start(f32[16]{0:T(128)} %param.18) | copy-start | bytes 196
  6.5 5.7 %copy-start.5 = (bf16[128,720]{0,1:T(8,128)(2,1)S(1)}, bf16[128,720]{0,1:T(8,128)(2,1)}, u32[]{:S(2)}) copy-start(bf16[128,720]{0,1:T(8,128)(2,1)} %param.14) | copy-start | bytes 552964
  6.5 5.8 %copy-start.11 = (s32[8]{0:T(128)S(1)}, s32[8]{0:T(128)}, u32[]{:S(2)}) copy-start(s32[8]{0:T(128)} %param.20) | copy-start | bytes 100
  6.5 5.8 %copy-start.12 = (s32[8]{0:T(128)S(1)}, s32[8]{0:T(128)}, u32[]{:S(2)}) copy-start(s32[8]{0:T(128)} %param.19) | copy-start | bytes 100
  6.5 82.9 %all-gather.4.cloned.1.call-start = ((), (), s32[]{:S(2)}) async-start(), calls=%async_computation.6 | async-start | bytes 2129920 | tf_op jit(solution)/shard_map/all_gather | solution.py:69
  8.1 127.7 %reduce-scatter.3.cloned.1.call-start = ((), (), s32[]{:S(2)}) async-start(), calls=%async_computation.7 | async-start | bytes 1843200 | tf_op jit(solution)/shard_map/reduce_scatter | solution.py:130
  95.2 3.0 copy-start.3
  98.3 2.2 copy-start
  100.5 1.8 copy-start.2
  100.5 2.2 copy-start.6
  103.8 5.6 %copy-start.9 = (s32[128,4]{0,1:T(4,128)S(1)}, s32[128,4]{0,1:T(4,128)}, u32[]{:S(2)}) copy-start(s32[128,4]{0,1:T(4,128)} %param.22) | copy-start | bytes 6148
  103.8 10.4 %copy-start.13 = (s32[64]{0:T(128)S(1)}, s32[64]{0:T(128)}, u32[]{:S(2)}) copy-start(s32[64]{0:T(128)} %param.21) | copy-start | bytes 772
  109.4 121.1 %all-gather.6.cloned.1.call-start = ((), (), s32[]{:S(2)}) async-start(), calls=%async_computation.9 | async-start | bytes 5898240 | tf_op jit(solution)/shard_map/all_gather | solution.py:161
  179.6 182.3 %reduce-scatter.5.cloned.1.call-start = ((), (), s32[]{:S(2)}) async-start(), calls=%async_computation.8 | async-start | bytes 11059200 | tf_op jit(solution)/shard_map/reduce_scatter | solution.py:183
  230.4 11.1 %copy-start.8 = (f32[2880]{0:T(1024)S(1)}, f32[2880]{0:T(1024)}, u32[]{:S(2)}) copy-start(f32[2880]{0:T(1024)} %param.24) | copy-start | bytes 34564
  230.4 14.5 %collective-permute-start.1 = (bf16[4,32,24,720]{3,2,1,0:T(8,128)(2,1)}, bf16[4,32,24,720]{3,2,1,0:T(8,128)(2,1)}, u32[]{:S(2)}, u32[]{:S(2)}) collective-permute-start(bf16[4,32,24,720]{3,2,1,0:T(8,128)(2,1)} %bitcast.167), channel_id=1, source_target_pairs={{0,4},{4,0},{1,5},{5,1},{2,6},{6,2},{3,7},{7,3},{8,12},{12,8},{9,1... | collective-permute-start | bytes 13271048 | tf_op jit(solution)/shard_map/ppermute | solution.py:162
  255.6 11.3 %copy-start.1 = (bf16[4,64,24,720]{3,2,1,0:T(8,128)(2,1)}, bf16[4,64,24,720]{3,2,1,0:T(8,128)(2,1)S(1)}, u32[]{:S(2)}) copy-start(bf16[4,64,24,720]{3,2,1,0:T(8,128)(2,1)S(1)} %pad_maximum_fusion) | copy-start | bytes 26542084
  274.3 0.7 copy-start.7
  296.5 1.2 collective-permute-start
  377.3 12.8 %collective-permute-start.2 = (bf16[32,24,720]{2,1,0:T(8,128)(2,1)}, bf16[32,24,720]{2,1,0:T(8,128)(2,1)}, u32[]{:S(2)}, u32[]{:S(2)}) collective-permute-start(bf16[32,24,720]{2,1,0:T(8,128)(2,1)} %gather_fusion.6), channel_id=1, source_target_pairs={{0,4},{4,0},{1,5},{5,1},{2,6},{6,2},{3,7},{7,3},{8,12},{12,8},{9,1... | collective-permute-start | bytes 3317768 | tf_op jit(solution)/shard_map/ppermute | solution.py:207
  379.2 18.6 %all-to-all-start.1 = ((f32[32,1,24]{2,1,0:T(1,128)}), f32[32,1,24]{2,1,0:T(1,128)}, u32[]{:S(2)}, u32[]{:S(2)}) async-start(f32[32,1,24]{2,1,0:T(1,128)} %bitcast.8), calls=%async_computation.1 | async-start | bytes 32768 | tf_op jit(solution)/shard_map/all_to_all | solution.py:211
  397.8 35.7 %all-to-all-start.3 = ((bf16[32,24,720]{2,1,0:T(8,128)(2,1)}), bf16[32,24,720]{2,1,0:T(8,128)(2,1)S(1)}, u32[]{:S(2)}, u32[]{:S(2)}) async-start(bf16[32,24,720]{2,1,0:T(8,128)(2,1)} %add_convert_fusion), calls=%async_computation.5 | async-start | bytes 2359296 | tf_op jit(solution)/shard_map/all_to_all | solution.py:210
Sparse Core Ops, SparseCore 0:
  10.1 79.3 all-gather.3
  109.5 26.2 reduce-scatter.2
  179.7 50.6 all-gather.5
  274.5 87.4 reduce-scatter.4
